TPU v7x, 512 devices: a whole 4x8x8 slice. The times are simulated.
512 devices in a mesh: obs: 32 (over y, z_lo), gr: 4 (over x), gc: 4 (over z_hi, core).
Axes of the slice: x: 4, y: 8, z: 8 (z_hi: 2, z_lo: 4; z = z_hi * 4 + z_lo), core: 2. Of those that a mesh axis runs over, the one named last changes fastest.
Arguments:
- legendre: float32 [4, 256, 8192], P(None, 'obs'), may hold values from -6 to 6
- longitude: float32 [4, 256], P(None, 'obs'), may hold values from -3.140625 to 3.140625
- orders: int32 [8192], replicated, may hold values from 0 to 360, as said below
- whitening: float32 [4, 256, 256], replicated, as said below
Outputs:
- normal: float32 [16384, 16384], P('obs', ('gr', 'gc'))
Inputs may be any that keep to these rules, and one draw needn't show every extreme that they name: The orders of 8192 degree-order pairs that follow one another cyclically in the order-major ordering of a degree-360 field (order m holds degrees m to 360); the run passes from the last pair, of order 360, to the first, of order 0, so the orders rise, fall once from 360 to 0, and rise again. Each arc's whitening matrix is lower triangular with a positive diagonal.
All inputs are finite; a program needn't handle non-finite values.
Results may differ from a plain program's by a relative error of at most 0.0003.
Values sent between devices are 32-bit elements; how exact they have to be, the bound alone decides.
No kernel may reach another device: no remote copies, remote signals or barrier semaphores. Data moves between devices by JAX's collectives and lax.ppermute only.
A program may use at most 64 MiB of HBM per device.

v0:
```python
import jax
import jax.numpy as jnp
from jax import lax
from jax.sharding import PartitionSpec as P

highest = lax.Precision.HIGHEST


def trig_design(values, longitudes, order_values):
    angles = order_values * longitudes
    stacked = jnp.stack([values * jnp.cos(angles), values * jnp.sin(angles)], axis=-1)
    return stacked.reshape(values.shape[:-1] + (2 * values.shape[-1],))


def whiten(design, matrices):
    return jnp.einsum("kec,kfe->kcf", design, matrices, precision=highest)


def shards(legendre, longitude, orders, whitening):
    arcs_total, epochs_local, pairs_total = legendre.shape
    arc_length = whitening.shape[1]
    obs_count = lax.axis_size("obs")
    grid_count = lax.axis_size(("gr", "gc"))
    grid_position = lax.axis_index(("gr", "gc"))
    row_pairs = pairs_total // obs_count
    col_pairs = pairs_total // grid_count
    row_piece = row_pairs // grid_count
    order_values = orders.astype(jnp.float32)
    accumulated = jnp.zeros((2 * row_pairs, 2 * col_pairs), jnp.float32)
    for arc_index in range(arcs_total):
        values = legendre[arc_index : arc_index + 1]
        longitudes = longitude[arc_index : arc_index + 1]
        matrices = whitening[arc_index : arc_index + 1]
        batch = values.shape[0]
        col_values = lax.dynamic_slice_in_dim(values, grid_position * col_pairs, col_pairs, 2)
        col_orders = lax.dynamic_slice_in_dim(order_values, grid_position * col_pairs, col_pairs, 0)
        value_rows = lax.all_gather(col_values, "obs", axis=1, tiled=True)
        longitude_rows = lax.all_gather(longitudes, "obs", axis=1, tiled=True)
        design = trig_design(value_rows, longitude_rows[:, :, None], col_orders)
        col_panel = jnp.einsum("kec,kfe->kcf", design, matrices, precision=highest)
        grouped = values.reshape(batch, epochs_local, obs_count, grid_count, row_piece)
        row_values = lax.dynamic_index_in_dim(grouped, grid_position, 3, keepdims=False)
        row_orders = lax.dynamic_index_in_dim(
            order_values.reshape(obs_count, grid_count, row_piece), grid_position, 1, keepdims=False
        )
        outgoing = trig_design(row_values, longitudes[:, :, None, None], row_orders)
        arrived = lax.all_to_all(outgoing, "obs", split_axis=2, concat_axis=1, tiled=True)
        own_rows = whiten(arrived.reshape(batch, arc_length, 2 * row_piece), matrices)
        accumulated = accumulated + jnp.einsum(
            "kcf,kdf->cd",
            lax.all_gather(own_rows, ("gr", "gc"), axis=1, tiled=True),
            col_panel,
            precision=highest,
        )
    return accumulated


def solution(mesh):
    placed = (P(None, "obs", None), P(None, "obs"), P(), P())
    return jax.shard_map(
        shards, mesh=mesh, in_specs=placed, out_specs=P("obs", ("gr", "gc")), check_vma=False
    )
```

profile of v0, /device:TPU:1, one launch (start us, length us, event | category | flops | bytes accessed | tf_op | source)
XLA Modules:
  0.0 630.3 jit_solution(18091526618583735605)
XLA Ops:
  2.0 2.0 reshape.715
  4.1 1.5 constant_dynamic-slice_fusion.1
  8.2 2.0 reshape.702
  10.2 1.5 constant_dynamic-slice_fusion.5
  12.0 2.5 fusion.50
  15.5 13.6 %all-to-all-start.2 = ((f32[32,1,256]{2,1,0:T(1,128)}), f32[32,1,256]{2,1,0:T(1,128)}, u32[]{:S(2)}, u32[]{:S(2)}) async-start(f32[32,1,256]{2,1,0:T(1,128)} %reshape.759), calls=%async_computation.2 | async-start | bytes 65536 | tf_op jit(solution)/shard_map/all_to_all | solution.py:47
  29.8 67.4 %all_gather.57 = f32[1,256,512]{2,1,0:T(8,128)S(1)} all-gather(f32[1,8,512]{2,1,0:T(8,128)S(1)} %constant_dynamic-slice_fusion), channel_id=1, replica_groups=mesh['obs'=32,'gr'=4,'gc'=4] {'obs'}, dimensions={1}, use_global_device_ids=true | all-gather | bytes 540672 | tf_op jit(solution)/shard_map/all_gather | solution.py:37
  99.6 62.2 %all_gather.49 = f32[1,256,512]{2,1,0:T(8,128)S(1)} all-gather(f32[1,8,512]{2,1,0:T(8,128)S(1)} %constant_dynamic-slice_fusion.4), channel_id=1, replica_groups=mesh['obs'=32,'gr'=4,'gc'=4] {'obs'}, dimensions={1}, use_global_device_ids=true | all-gather | bytes 540672 | tf_op jit(solution)/shard_map/all_gather | solution.py:37
  161.8 64.1 %all_gather.53 = f32[1,256,512]{2,1,0:T(8,128)S(1)} all-gather(f32[1,8,512]{2,1,0:T(8,128)S(1)} %constant_dynamic-slice_fusion.2), channel_id=1, replica_groups=mesh['obs'=32,'gr'=4,'gc'=4] {'obs'}, dimensions={1}, use_global_device_ids=true | all-gather | bytes 540672 | tf_op jit(solution)/shard_map/all_gather | solution.py:37
  225.9 62.3 %all_gather.45 = f32[1,256,512]{2,1,0:T(8,128)S(1)} all-gather(f32[1,8,512]{2,1,0:T(8,128)S(1)} %constant_dynamic-slice_fusion.6), channel_id=1, replica_groups=mesh['obs'=32,'gr'=4,'gc'=4] {'obs'}, dimensions={1}, use_global_device_ids=true | all-gather | bytes 540672 | tf_op jit(solution)/shard_map/all_gather | solution.py:37
  288.2 62.8 %all-reduce.4 = (f32[256]{0:T(256)S(1)}, f32[256]{0:T(256)S(1)}, f32[256]{0:T(256)S(1)}, f32[256]{0:T(256)S(1)}) all-reduce(f32[256]{0:T(256)S(1)} %fusion.54, f32[256]{0:T(256)S(1)} %fusion.52, f32[256]{0:T(256)S(1)} %fusion.53, f32[256]{0:T(256)S(1)} %fusion.55), channel_id=1, replica_groups=mesh['obs'=32,'gr'=4,'gc'=4] {'obs'}, use_global_device_ids=true, to_apply=%add.2 | all-reduce | flops 1024 | bytes 8192
  351.0 8.8 %fusion.13 = (f32[1,256,512,1]{2,1,3,0:T(8,128)S(1)}, f32[1,256,512,1]{2,1,3,0:T(8,128)S(1)}, f32[1,256,512,1]{2,1,3,0:T(8,128)S(1)}, f32[1,256,512,1]{2,1,3,0:T...) fusion(f32[1,256,512]{2,1,0:T(8,128)S(1)} %all_gather.57, ...), kind=kLoop, calls=%fused_computation.26 | loop fusion | flops 1572864 | bytes 6297600 | tf_op jit(solution)/shard_map/stack | solution.py:11
  363.3 2.7 pad_maximum_fusion
  366.0 1.6 copy.58
  367.6 1.7 reshape.708
  372.5 1.5 copy.62
  374.1 1.7 reshape.714
  375.8 2.3 fusion.24
  378.1 2.3 copy.70
  380.3 2.9 reshape.726
  383.2 3.3 fusion.16
  387.5 4.3 all-to-all-start
  395.2 108.4 %all-gather.2 = f32[512,256]{1,0:T(8,128)} all-gather(f32[32,256]{1,0:T(8,128)S(1)} %fusion.22), channel_id=4, replica_groups=mesh['obs'=32,'gr'=4,'gc'=4] {'gr','gc'}, dimensions={0}, use_global_device_ids=true | all-gather | bytes 557056 | tf_op jit(solution)/shard_map/all_gather | solution.py:51
  503.6 7.2 %all-to-all-start.1 = ((f32[32,1,256]{2,1,0:T(1,128)}), f32[32,1,256]{2,1,0:T(1,128)S(1)}, u32[]{:S(2)}, u32[]{:S(2)}) async-start(f32[32,1,256]{2,1,0:T(1,128)} %reshape.763), calls=%async_computation.1 | async-start | bytes 65536 | tf_op jit(solution)/shard_map/all_to_all | solution.py:47
  512.9 28.4 %all-gather = f32[512,256]{1,0:T(8,128)} all-gather(f32[32,256]{1,0:T(8,128)S(1)} %fusion.30), channel_id=2, replica_groups=mesh['obs'=32,'gr'=4,'gc'=4] {'gr','gc'}, dimensions={0}, use_global_device_ids=true | all-gather | bytes 557056 | tf_op jit(solution)/shard_map/all_gather | solution.py:51
  541.3 10.0 %all-to-all-start.3 = ((f32[32,1,256]{2,1,0:T(1,128)}), f32[32,1,256]{2,1,0:T(1,128)S(1)}, u32[]{:S(2)}, u32[]{:S(2)}) async-start(f32[32,1,256]{2,1,0:T(1,128)} %reshape.765), calls=%async_computation.3 | async-start | bytes 65536 | tf_op jit(solution)/shard_map/all_to_all | solution.py:47
  553.4 37.7 %all-gather.1 = f32[512,256]{1,0:T(8,128)} all-gather(f32[32,256]{1,0:T(8,128)S(1)} %fusion.26), channel_id=3, replica_groups=mesh['obs'=32,'gr'=4,'gc'=4] {'gr','gc'}, dimensions={0}, use_global_device_ids=true | all-gather | bytes 557056 | tf_op jit(solution)/shard_map/all_gather | solution.py:51
  593.2 26.7 %all-gather.3 = f32[512,256]{1,0:T(8,128)S(1)} all-gather(f32[32,256]{1,0:T(8,128)S(1)} %fusion.18), channel_id=5, replica_groups=mesh['obs'=32,'gr'=4,'gc'=4] {'gr','gc'}, dimensions={0}, use_global_device_ids=true | all-gather | bytes 557056 | tf_op jit(solution)/shard_map/all_gather | solution.py:51
  620.0 2.9 fusion.63
  622.9 1.9 fusion.61
  624.8 1.9 fusion.62
  626.7 3.6 add_add_fusion
  (84 shorter events, 25.4 us)
Async XLA Ops:
  2.0 4.3 copy-start.8
  2.0 4.9 copy-start.7
  6.9 0.6 copy-start.6
  11.7 87.5 %copy-start.9 = (f32[4,8]{1,0:T(4,128)S(1)}, f32[4,8]{1,0:T(4,128)}, u32[]{:S(2)}) copy-start(f32[4,8]{1,0:T(4,128)} %param.5) | copy-start | bytes 388
  15.5 372.0 %all-to-all-start.2 = ((f32[32,1,256]{2,1,0:T(1,128)}), f32[32,1,256]{2,1,0:T(1,128)}, u32[]{:S(2)}, u32[]{:S(2)}) async-start(f32[32,1,256]{2,1,0:T(1,128)} %reshape.759), calls=%async_computation.2 | async-start | bytes 65536 | tf_op jit(solution)/shard_map/all_to_all | solution.py:47
  361.0 1.3 copy-start.5
  366.0 3.4 copy-start.1
  369.3 1.2 copy-start.2
  387.5 116.2 %all-to-all-start = ((f32[32,1,256]{2,1,0:T(1,128)}), f32[32,1,256]{2,1,0:T(1,128)S(1)}, u32[]{:S(2)}, u32[]{:S(2)}) async-start(f32[32,1,256]{2,1,0:T(1,128)} %reshape.761), calls=%async_computation | async-start | bytes 65536 | tf_op jit(solution)/shard_map/all_to_all | solution.py:47
  503.6 37.6 %all-to-all-start.1 = ((f32[32,1,256]{2,1,0:T(1,128)}), f32[32,1,256]{2,1,0:T(1,128)S(1)}, u32[]{:S(2)}, u32[]{:S(2)}) async-start(f32[32,1,256]{2,1,0:T(1,128)} %reshape.763), calls=%async_computation.1 | async-start | bytes 65536 | tf_op jit(solution)/shard_map/all_to_all | solution.py:47
  541.3 49.9 %all-to-all-start.3 = ((f32[32,1,256]{2,1,0:T(1,128)}), f32[32,1,256]{2,1,0:T(1,128)S(1)}, u32[]{:S(2)}, u32[]{:S(2)}) async-start(f32[32,1,256]{2,1,0:T(1,128)} %reshape.765), calls=%async_computation.3 | async-start | bytes 65536 | tf_op jit(solution)/shard_map/all_to_all | solution.py:47
  593.2 29.7 %copy-start.3 = (f32[512,256]{1,0:T(8,128)S(1)}, f32[512,256]{1,0:T(8,128)}, u32[]{:S(2)}) copy-start(f32[512,256]{1,0:T(8,128)} %all-gather) | copy-start | bytes 1572868
  622.9 1.9 copy-start.4
  624.8 1.9 copy-start
where the time goes:
time: 631 us; the launch traced here: 630 us
  blocking collectives  520 us (82%)
  starting transfers between devices  35.1 us (6%)
  local copies, waits for them, and re-layouts  32.2 us (5%)
  matrix products  23 us (4%)
  other arithmetic  18.8 us (3%)
    all_gather x4, blocking collectives, shards(): value_rows = lax.all_gather(col_values, 'obs', axis=1, tiled=True)  256 us
    all_gather x4, blocking collectives, shards(): lax.all_gather(own_rows, ('gr', 'gc'), axis=1, tiled=True)  201 us
    unnamed x1, blocking collectives  62.8 us
    all_to_all x4, starting transfers between devices, shards(): lax.all_to_all(outgoing, 'obs', split_axis=2, concat_axis=1, tiled=True)  35.1 us
    another operation x7, other arithmetic, trig_design(): jnp.stack([values * jnp.cos(angles), values * jnp.sin(angles)], axis=-1)  12.7 us
  transfers between devices with their start and end apart: 4, of which 0 were waited for; matrix products, arithmetic and copies ran while one was open for 7% of the time, Pallas kernels for 0%

commit v1 on v0

--- a/solution.py
+++ b/solution.py
@@ -34,7 +34,15 @@
         batch = values.shape[0]
         col_values = lax.dynamic_slice_in_dim(values, grid_position * col_pairs, col_pairs, 2)
         col_orders = lax.dynamic_slice_in_dim(order_values, grid_position * col_pairs, col_pairs, 0)
-        value_rows = lax.all_gather(col_values, "obs", axis=1, tiled=True)
+        value_rows = jnp.concatenate(
+            lax.all_to_all(
+                jnp.stack([col_values for _ in range(lax.axis_size("obs"))], axis=0),
+                axis_name="obs",
+                split_axis=0,
+                concat_axis=0,
+            ),
+            axis=1,
+        )
         longitude_rows = lax.all_gather(longitudes, "obs", axis=1, tiled=True)
         design = trig_design(value_rows, longitude_rows[:, :, None], col_orders)
         col_panel = jnp.einsum("kec,kfe->kcf", design, matrices, precision=highest)

time: 631 us -> 393 us (0.62)
  the two profiles are of different devices: /device:TPU:1 before, /device:TPU:33 now
where the time goes in v1:
time: 393 us; the launch traced here: 392 us
  blocking collectives  228 us (58%)
  starting transfers between devices  68.8 us (18%)
  waiting for transfers between devices  32.2 us (8%)
  local copies, waits for them, and re-layouts  27.9 us (7%)
  matrix products  18.7 us (5%)
  other arithmetic  15.4 us (4%)
    all_gather x4, blocking collectives, shards(): lax.all_gather(own_rows, ('gr', 'gc'), axis=1, tiled=True)  163 us
    unnamed x1, blocking collectives  65.6 us
    all_to_all x4, starting transfers between devices, shards(): lax.all_to_all(outgoing, 'obs', split_axis=2, concat_axis=1, tiled=True)  37.5 us
    all_to_all x4, starting transfers between devices, shards(): lax.all_to_all(jnp.stack([col_values for _ in range(lax.axis_size('obs'))...  31.3 us
    all_to_all x4, waiting for transfers between devices, shards(): lax.all_to_all(jnp.stack([col_values for _ in range(lax.axis_size('obs'))...  17 us
    all_to_all x4, waiting for transfers between devices, shards(): lax.all_to_all(outgoing, 'obs', split_axis=2, concat_axis=1, tiled=True)  15.2 us
    mul x2, other arithmetic, trig_design(): values * jnp.cos(angles)  9.87 us
    dot_general x4, matrix products, shards(): jnp.einsum('kcf,kdf->cd', lax.all_gather(own_rows, ('gr', 'gc'), axis=1,...  9.26 us
  transfers between devices with their start and end apart: 8, of which 6 were waited for; matrix products, arithmetic and copies ran while one was open for 2% of the time, Pallas kernels for 0%

profile of v1, /device:TPU:33, one launch (start us, length us, event | category | flops | bytes accessed | tf_op | source)
XLA Modules:
  0.0 392.4 jit_solution(8561155025694034372)
XLA Ops:
  7.3 12.2 %all-to-all-start.2 = ((f32[32,1,256]{2,1,0:T(1,128)}), f32[32,1,256]{2,1,0:T(1,128)S(1)}, u32[]{:S(2)}, u32[]{:S(2)}) async-start(f32[32,1,256]{2,1,0:T(1,128)} %reshape.959), calls=%async_computation.2 | async-start | bytes 65536 | tf_op jit(solution)/shard_map/all_to_all | solution.py:55
  20.5 3.7 all-to-all-done.2
  24.2 8.3 %all-to-all-start = ((f32[32,1,256]{2,1,0:T(1,128)}), f32[32,1,256]{2,1,0:T(1,128)S(1)}, u32[]{:S(2)}, u32[]{:S(2)}) async-start(f32[32,1,256]{2,1,0:T(1,128)} %reshape.957), calls=%async_computation | async-start | bytes 65536 | tf_op jit(solution)/shard_map/all_to_all | solution.py:55
  33.4 3.7 all-to-all-done
  37.1 8.4 %all-to-all-start.4 = ((f32[32,1,256]{2,1,0:T(1,128)}), f32[32,1,256]{2,1,0:T(1,128)S(1)}, u32[]{:S(2)}, u32[]{:S(2)}) async-start(f32[32,1,256]{2,1,0:T(1,128)} %reshape.955), calls=%async_computation.4 | async-start | bytes 65536 | tf_op jit(solution)/shard_map/all_to_all | solution.py:55
  46.5 3.4 all-to-all-done.4
  49.9 8.6 %all-to-all-start.6 = ((f32[32,1,256]{2,1,0:T(1,128)}), f32[32,1,256]{2,1,0:T(1,128)S(1)}, u32[]{:S(2)}, u32[]{:S(2)}) async-start(f32[32,1,256]{2,1,0:T(1,128)} %reshape.961), calls=%async_computation.6 | async-start | bytes 65536 | tf_op jit(solution)/shard_map/all_to_all | solution.py:55
  58.5 4.4 %all-to-all-done.6 = f32[32,1,256]{2,1,0:T(1,128)S(1)} async-done(((f32[32,1,256]{2,1,0:T(1,128)}), f32[32,1,256]{2,1,0:T(1,128)S(1)}, u32[]{:S(2)}, u32[]{:S(2)}) %all-to-all-start.6) | async-done | bytes 32800 | tf_op jit(solution)/shard_map/all_to_all | solution.py:55
  63.7 8.7 %all-to-all-start.1 = ((f32[32,1,8,512]{3,2,1,0:T(8,128)}), f32[32,1,8,512]{3,2,1,0:T(8,128)S(1)}, u32[]{:S(2)}, u32[]{:S(2)}) async-start(f32[32,1,8,512]{3,2,1,0:T(8,128)} %stack.25), calls=%async_computation.1 | async-start | bytes 1048576 | tf_op jit(solution)/shard_map/all_to_all | solution.py:38
  72.5 9.6 %all-to-all-done.1 = f32[32,1,8,512]{3,2,1,0:T(8,128)S(1)} async-done(((f32[32,1,8,512]{3,2,1,0:T(8,128)}), f32[32,1,8,512]{3,2,1,0:T(8,128)S(1)}, u32[]{:S(2)}, u32[]{:S(2)}) %all-to-all-start.1) | async-done | bytes 524320 | tf_op jit(solution)/shard_map/all_to_all | solution.py:38
  83.0 7.9 %all-to-all-start.3 = ((f32[32,1,8,512]{3,2,1,0:T(8,128)}), f32[32,1,8,512]{3,2,1,0:T(8,128)S(1)}, u32[]{:S(2)}, u32[]{:S(2)}) async-start(f32[32,1,8,512]{3,2,1,0:T(8,128)} %stack.28), calls=%async_computation.3 | async-start | bytes 1048576 | tf_op jit(solution)/shard_map/all_to_all | solution.py:38
  93.2 7.4 %all-to-all-done.3 = f32[32,1,8,512]{3,2,1,0:T(8,128)S(1)} async-done(((f32[32,1,8,512]{3,2,1,0:T(8,128)}), f32[32,1,8,512]{3,2,1,0:T(8,128)S(1)}, u32[]{:S(2)}, u32[]{:S(2)}) %all-to-all-start.3) | async-done | bytes 524320 | tf_op jit(solution)/shard_map/all_to_all | solution.py:38
  101.4 7.9 %all-to-all-start.5 = ((f32[32,1,8,512]{3,2,1,0:T(8,128)}), f32[32,1,8,512]{3,2,1,0:T(8,128)S(1)}, u32[]{:S(2)}, u32[]{:S(2)}) async-start(f32[32,1,8,512]{3,2,1,0:T(8,128)} %stack.31), calls=%async_computation.5 | async-start | bytes 1048576 | tf_op jit(solution)/shard_map/all_to_all | solution.py:38
  109.4 65.6 %all-reduce.4 = (f32[256]{0:T(256)S(1)}, f32[256]{0:T(256)S(1)}, f32[256]{0:T(256)S(1)}, f32[256]{0:T(256)S(1)}) all-reduce(f32[256]{0:T(256)S(1)} %fusion.46, f32[256]{0:T(256)S(1)} %fusion.44, f32[256]{0:T(256)S(1)} %fusion.45, f32[256]{0:T(256)S(1)} %fusion.47), channel_id=1, replica_groups=mesh['obs'=32,'gr'=4,'gc'=4] {'obs'}, use_global_device_ids=true, to_apply=%add.2 | all-reduce | flops 1024 | bytes 8192
  180.7 6.8 %all-to-all-start.7 = ((f32[32,1,8,512]{3,2,1,0:T(8,128)}), f32[32,1,8,512]{3,2,1,0:T(8,128)S(1)}, u32[]{:S(2)}, u32[]{:S(2)}) async-start(f32[32,1,8,512]{3,2,1,0:T(8,128)} %stack.34), calls=%async_computation.7 | async-start | bytes 1048576 | tf_op jit(solution)/shard_map/all_to_all | solution.py:38
  187.8 59.1 %all-gather.1 = f32[512,256]{1,0:T(8,128)} all-gather(f32[32,256]{1,0:T(8,128)S(1)} %fusion.18), channel_id=3, replica_groups=mesh['obs'=32,'gr'=4,'gc'=4] {'gr','gc'}, dimensions={0}, use_global_device_ids=true | all-gather | bytes 557056 | tf_op jit(solution)/shard_map/all_gather | solution.py:59
  246.9 36.6 %all-gather = f32[512,256]{1,0:T(8,128)} all-gather(f32[32,256]{1,0:T(8,128)S(1)} %fusion.22), channel_id=2, replica_groups=mesh['obs'=32,'gr'=4,'gc'=4] {'gr','gc'}, dimensions={0}, use_global_device_ids=true | all-gather | bytes 557056 | tf_op jit(solution)/shard_map/all_gather | solution.py:59
  283.5 28.2 %all-gather.2 = f32[512,256]{1,0:T(8,128)} all-gather(f32[32,256]{1,0:T(8,128)S(1)} %fusion.14), channel_id=4, replica_groups=mesh['obs'=32,'gr'=4,'gc'=4] {'gr','gc'}, dimensions={0}, use_global_device_ids=true | all-gather | bytes 557056 | tf_op jit(solution)/shard_map/all_gather | solution.py:59
  311.7 38.8 %all-gather.3 = f32[512,256]{1,0:T(8,128)} all-gather(f32[32,256]{1,0:T(8,128)S(1)} %fusion.10), channel_id=5, replica_groups=mesh['obs'=32,'gr'=4,'gc'=4] {'gr','gc'}, dimensions={0}, use_global_device_ids=true | all-gather | bytes 557056 | tf_op jit(solution)/shard_map/all_gather | solution.py:59
  350.5 8.9 %fusion.6 = (f32[1,256,512,1]{2,1,3,0:T(8,128)}, f32[1,256,512,1]{2,1,3,0:T(8,128)}, f32[1,256,512,1]{2,1,3,0:T(8,128)S(1)}, f32[1,256,512,1]{2,1,3,0:T(8,128)S(...) fusion(f32[32,1,8,512]{3,2,1,0:T(8,128)S(1)} %all-to-all-done.7, ...), kind=kLoop, calls=%fused_computation.19 | loop fusion | flops 1572864 | bytes 6297600 | tf_op jit(solution)/shard_map/mul | solution.py:11
  362.8 1.5 copy.54
  364.3 1.7 reshape.901
  366.0 2.4 fusion.20
  371.5 1.7 reshape.915
  373.2 2.3 fusion.12
  375.5 2.3 copy.66
  377.8 2.9 reshape.922
  380.7 2.4 fusion.8
  383.1 1.9 fusion.54
  385.0 1.9 fusion.53
  386.9 1.9 fusion.55
  388.8 3.6 add_add_fusion
  (94 shorter events, 26.7 us)
Async XLA Ops:
  0.0 1.3 copy-start.9
  3.9 1.4 copy-start.10
  7.3 16.9 %all-to-all-start.2 = ((f32[32,1,256]{2,1,0:T(1,128)}), f32[32,1,256]{2,1,0:T(1,128)S(1)}, u32[]{:S(2)}, u32[]{:S(2)}) async-start(f32[32,1,256]{2,1,0:T(1,128)} %reshape.959), calls=%async_computation.2 | async-start | bytes 65536 | tf_op jit(solution)/shard_map/all_to_all | solution.py:55
  24.2 12.9 %all-to-all-start = ((f32[32,1,256]{2,1,0:T(1,128)}), f32[32,1,256]{2,1,0:T(1,128)S(1)}, u32[]{:S(2)}, u32[]{:S(2)}) async-start(f32[32,1,256]{2,1,0:T(1,128)} %reshape.957), calls=%async_computation | async-start | bytes 65536 | tf_op jit(solution)/shard_map/all_to_all | solution.py:55
  37.1 12.8 %all-to-all-start.4 = ((f32[32,1,256]{2,1,0:T(1,128)}), f32[32,1,256]{2,1,0:T(1,128)S(1)}, u32[]{:S(2)}, u32[]{:S(2)}) async-start(f32[32,1,256]{2,1,0:T(1,128)} %reshape.955), calls=%async_computation.4 | async-start | bytes 65536 | tf_op jit(solution)/shard_map/all_to_all | solution.py:55
  49.9 13.0 %all-to-all-start.6 = ((f32[32,1,256]{2,1,0:T(1,128)}), f32[32,1,256]{2,1,0:T(1,128)S(1)}, u32[]{:S(2)}, u32[]{:S(2)}) async-start(f32[32,1,256]{2,1,0:T(1,128)} %reshape.961), calls=%async_computation.6 | async-start | bytes 65536 | tf_op jit(solution)/shard_map/all_to_all | solution.py:55
  63.7 18.4 %all-to-all-start.1 = ((f32[32,1,8,512]{3,2,1,0:T(8,128)}), f32[32,1,8,512]{3,2,1,0:T(8,128)S(1)}, u32[]{:S(2)}, u32[]{:S(2)}) async-start(f32[32,1,8,512]{3,2,1,0:T(8,128)} %stack.25), calls=%async_computation.1 | async-start | bytes 1048576 | tf_op jit(solution)/shard_map/all_to_all | solution.py:38
  72.5 106.2 %copy-start = (f32[4,256,256]{2,1,0:T(8,128)S(1)}, f32[4,256,256]{2,1,0:T(8,128)}, u32[]{:S(2)}) copy-start(f32[4,256,256]{2,1,0:T(8,128)} %param.7) | copy-start | bytes 3145732
  83.0 17.6 %all-to-all-start.3 = ((f32[32,1,8,512]{3,2,1,0:T(8,128)}), f32[32,1,8,512]{3,2,1,0:T(8,128)S(1)}, u32[]{:S(2)}, u32[]{:S(2)}) async-start(f32[32,1,8,512]{3,2,1,0:T(8,128)} %stack.28), calls=%async_computation.3 | async-start | bytes 1048576 | tf_op jit(solution)/shard_map/all_to_all | solution.py:38
  101.4 78.4 %all-to-all-start.5 = ((f32[32,1,8,512]{3,2,1,0:T(8,128)}), f32[32,1,8,512]{3,2,1,0:T(8,128)S(1)}, u32[]{:S(2)}, u32[]{:S(2)}) async-start(f32[32,1,8,512]{3,2,1,0:T(8,128)} %stack.31), calls=%async_computation.5 | async-start | bytes 1048576 | tf_op jit(solution)/shard_map/all_to_all | solution.py:38
  180.7 169.8 %all-to-all-start.7 = ((f32[32,1,8,512]{3,2,1,0:T(8,128)}), f32[32,1,8,512]{3,2,1,0:T(8,128)S(1)}, u32[]{:S(2)}, u32[]{:S(2)}) async-start(f32[32,1,8,512]{3,2,1,0:T(8,128)} %stack.34), calls=%async_computation.7 | async-start | bytes 1048576 | tf_op jit(solution)/shard_map/all_to_all | solution.py:38
  366.0 2.4 copy-start.5
  366.0 2.4 copy-start.6
  366.0 2.4 copy-start.7
  366.0 2.4 copy-start.8
  380.7 2.4 copy-start.4
  383.1 1.9 copy-start.3
  385.0 1.9 copy-start.2
  386.9 1.9 copy-start.1
